TPU v7x, 256 devices: a whole 4x4x8 slice. The times are simulated.
256 devices in a mesh: gz: 32 (over x, z), gx: 8 (over y, core).
Axes of the slice: x: 4, y: 4, z: 8, core: 2. Of those that a mesh axis runs over, the one named last changes fastest.
Arguments:
- u_field: bfloat16 [2, 512, 2048, 128], P(None, 'gx', 'gz'), may hold values from -64 to 64, as said below
- w_field: bfloat16 [2, 512, 2048, 128], P(None, 'gx', 'gz'), may hold values from -64 to 64, as said below
Outputs:
- modes: float32 [2, 512, 2048, 128], P(None, 'gx', 'gz')
- factor_r: float32 [2, 128, 128], replicated
Inputs may be any that keep to these rules, and one draw needn't show every extreme that they name: `u_field`: velocity values of a snapshot. `w_field`: velocity values of a snapshot.
All inputs are finite; a program needn't handle non-finite values.
Results may differ from a plain program's by a relative error of at most 0.0003.
Values may be sent and summed in bfloat16 or wider, within the bound.
No kernel may reach another device: no remote copies, remote signals or barrier semaphores. Data moves between devices by JAX's collectives and lax.ppermute only.
A program may use at most 64 MiB of HBM per device.

v0:
```python
import jax
import jax.numpy as jnp
from jax import lax
from jax.sharding import PartitionSpec as P

span_step = 0.75


def with_halo(cells, sides, width):
    for axis, dim in sides:
        count = lax.axis_size(axis)
        head = lax.slice_in_dim(cells, 0, width, axis=dim)
        tail = lax.slice_in_dim(cells, cells.shape[dim] - width, cells.shape[dim], axis=dim)
        cells = jnp.concatenate(
            [
                lax.ppermute(tail, axis, [(i, (i + 1) % count) for i in range(count)]),
                cells,
                lax.ppermute(head, axis, [((i + 1) % count, i) for i in range(count)]),
            ],
            axis=dim,
        )
    return cells


def local(u_field, w_field):
    planes, rows_x, rows_z, snaps = u_field.shape
    padded_u = with_halo(u_field, (("gz", 2),), 2).astype(jnp.float32)
    padded_w = with_halo(w_field, (("gx", 1),), 2).astype(jnp.float32)
    span_diff = 8.0 * (padded_u[:, :, 3:-1] - padded_u[:, :, 1:-3]) - (
        padded_u[:, :, 4:] - padded_u[:, :, :-4]
    )
    stream_diff = 8.0 * (padded_w[:, 3:-1] - padded_w[:, 1:-3]) - (
        padded_w[:, 4:] - padded_w[:, :-4]
    )
    vorticity = span_diff / (12.0 * span_step) - stream_diff / 12.0
    columns = vorticity.reshape(planes, rows_x * rows_z, snaps)
    gram_local = jnp.einsum(
        "pcs,pct->pst",
        columns,
        columns,
        precision=lax.Precision.HIGHEST,
        preferred_element_type=jnp.float32,
    )
    gram_sum = lax.psum(gram_local, ("gz", "gx"))
    total_cells = rows_x * rows_z * lax.axis_size("gz") * lax.axis_size("gx")
    gram = gram_sum / total_cells
    lower = jnp.linalg.cholesky(gram)
    identity_matrix = jnp.broadcast_to(jnp.eye(snaps, dtype=gram.dtype), lower.shape)
    lower_inverse = lax.linalg.triangular_solve(lower, identity_matrix, left_side=True, lower=True)
    inverse_r = jnp.transpose(lower_inverse, (0, 2, 1))
    modes = jnp.einsum(
        "pcs,pst->pct",
        columns,
        inverse_r,
        precision=lax.Precision.HIGHEST,
        preferred_element_type=jnp.float32,
    )
    modes = modes.reshape(planes, rows_x, rows_z, snaps)
    factor_r = jnp.transpose(lower, (0, 2, 1))
    return (modes, factor_r)


def solution(mesh):
    return jax.shard_map(
        local,
        mesh=mesh,
        in_specs=(P(None, "gx", "gz", None), P(None, "gx", "gz", None)),
        out_specs=(P(None, "gx", "gz", None), P()),
        check_vma=False,
    )
```

profile of v0, /device:TPU:2, one launch (start us, length us, event | category | flops | bytes accessed | tf_op | source)
XLA Modules:
  0.0 339.1 jit_solution(9191449530525586369)
XLA Ops:
  7.2 0.0 all-reduce.2.cloned.1.call-start
  7.2 1.3 fusion.13
  8.5 2.0 collective-permute-start
  10.5 4.0 %collective-permute-start.1 = (bf16[2,64,2,128]{3,2,1,0:T(2,128)(2,1)S(1)}, bf16[2,64,2,128]{3,2,1,0:T(2,128)(2,1)S(1)}, u32[]{:S(2)}, u32[]{:S(2)}) collective-permute-start(bf16[2,64,2,128]{3,2,1,0:T(2,128)(2,1)S(1)} %get-tuple-element.7), channel_id=1, source_target_pairs={{8,0},{16,8},{24,16},{32,24},{40,32},{48,40},{56,48},{64,56},{72,6... | collective-permute-start | bytes 196616 | tf_op jit(solution)/shard_map/ppermute | solution.py:18
  14.5 0.9 fusion.14
  15.4 0.0 collective-permute-start.2
  15.4 2.9 collective-permute-start.3
  18.4 2.8 maximum_convert_fusion
  21.2 0.3 maximum_convert_fusion.1
  21.6 2.8 fusion.2
  24.4 1.9 copy-done
  26.3 7.5 %fusion.15 = f32[2,128,128]{1,2,0:T(8,128)} fusion(f32[2,4096,128]{2,1,0:T(8,128)S(1)} %bitcast.17), kind=kOutput, calls=%fused_computation.29 | convolution fusion | flops 1610612736 | bytes 4325376 | tf_op jit(solution)/shard_map/pcs,pct->pst/dot_general | solution.py:37
  33.8 0.0 all-reduce.2.cloned.1.call-update
  33.9 245.2 %all-reduce.2.cloned.1.call-done = f32[2,128,128]{1,2,0:T(8,128)} async-done(((f32[2,128,128]{1,2,0:T(8,128)}), f32[2,128,128]{1,2,0:T(8,128)}) %all-reduce.2.cloned.1.call-update) | async-done | bytes 131088 | tf_op jit(solution)/shard_map/psum | solution.py:44
  279.1 0.9 broadcast_multiply_fusion
  280.0 0.1 copy.10
  280.1 0.9 fusion.9
  281.0 23.6 %custom-call.7 = f32[2,128,128]{2,1,0:T(8,128)S(1)} custom-call(f32[2,128,128]{2,1,0:T(8,128)S(1)} %fusion.9), custom_call_target="Cholesky" | custom-call | tf_op jit(solution)/shard_map/jit(cholesky)/cholesky | solution.py:47
  304.7 0.1 compare_reduce_fusion
  304.8 0.1 fusion.10
  304.9 19.7 %custom-call.8 = f32[2,1,128,128]{2,3,1,0:T(8,128)S(1)} custom-call(f32[2,1,128,128]{3,2,1,0:T(8,128)S(1)} %get-tuple-element.11), custom_call_target="InvertDiagBlocksLowerTriangular" | custom-call | tf_op jit(solution)/shard_map/triangular_solve | solution.py:49
  324.6 0.4 fusion.7
  325.0 6.5 %fusion.16 = f32[2,4096,128]{2,1,0:T(8,128)} fusion(f32[2,4096,128]{2,1,0:T(8,128)} %bitcast.18, f32[2,128,128]{2,1,0:T(8,128)S(1)} %fusion.7), kind=kOutput, calls=%fused_computation.30 | convolution fusion | flops 1610612736 | bytes 8519680 | tf_op jit(solution)/shard_map/pcs,pst->pct/dot_general | solution.py:51
  331.5 0.8 copy.11
  (11 shorter events, 0.1 us)
Async XLA Ops:
  7.2 14.1 %copy-start.1 = (bf16[2,64,64,128]{3,2,1,0:T(8,128)(2,1)S(1)}, bf16[2,64,64,128]{3,2,1,0:T(8,128)(2,1)}, u32[]{:S(2)}) copy-start(bf16[2,64,64,128]{3,2,1,0:T(8,128)(2,1)} %param.3) | copy-start | bytes 6291460
  7.2 271.9 %all-reduce.2.cloned.1.call-start = ((), (), s32[]{:S(2)}) async-start(), calls=%async_computation | async-start | bytes 262144 | tf_op jit(solution)/shard_map/psum | solution.py:44
  8.5 9.9 %collective-permute-start = (bf16[2,64,2,128]{3,2,1,0:T(2,128)(2,1)S(1)}, bf16[2,64,2,128]{3,2,1,0:T(2,128)(2,1)S(1)}, u32[]{:S(2)}, u32[]{:S(2)}) collective-permute-start(bf16[2,64,2,128]{3,2,1,0:T(2,128)(2,1)S(1)} %get-tuple-element.6), channel_id=1, source_target_pairs={{0,8},{8,16},{16,24},{24,32},{32,40},{40,48},{48,56},{56,64},{64,7... | collective-permute-start | bytes 196616 | tf_op jit(solution)/shard_map/ppermute | solution.py:16
  10.5 7.9 %collective-permute-start.1 = (bf16[2,64,2,128]{3,2,1,0:T(2,128)(2,1)S(1)}, bf16[2,64,2,128]{3,2,1,0:T(2,128)(2,1)S(1)}, u32[]{:S(2)}, u32[]{:S(2)}) collective-permute-start(bf16[2,64,2,128]{3,2,1,0:T(2,128)(2,1)S(1)} %get-tuple-element.7), channel_id=1, source_target_pairs={{8,0},{16,8},{24,16},{32,24},{40,32},{48,40},{56,48},{64,56},{72,6... | collective-permute-start | bytes 196616 | tf_op jit(solution)/shard_map/ppermute | solution.py:18
  15.4 5.8 %collective-permute-start.2 = (bf16[2,2,64,128]{3,2,1,0:T(8,128)(2,1)S(1)}, bf16[2,2,64,128]{3,2,1,0:T(8,128)(2,1)S(1)}, u32[]{:S(2)}, u32[]{:S(2)}) collective-permute-start(bf16[2,2,64,128]{3,2,1,0:T(8,128)(2,1)S(1)} %get-tuple-element.8), channel_id=1, source_target_pairs={{0,1},{1,2},{2,3},{3,4},{4,5},{5,6},{6,7},{7,0},{8,9},{9,10},{10,1... | collective-permute-start | bytes 196616 | tf_op jit(solution)/shard_map/ppermute | solution.py:16
  15.4 5.8 %collective-permute-start.3 = (bf16[2,2,64,128]{3,2,1,0:T(8,128)(2,1)S(1)}, bf16[2,2,64,128]{3,2,1,0:T(8,128)(2,1)S(1)}, u32[]{:S(2)}, u32[]{:S(2)}) collective-permute-start(bf16[2,2,64,128]{3,2,1,0:T(8,128)(2,1)S(1)} %get-tuple-element.9), channel_id=1, source_target_pairs={{1,0},{2,1},{3,2},{4,3},{5,4},{6,5},{7,6},{0,7},{9,8},{10,9},{11,1... | collective-permute-start | bytes 196616 | tf_op jit(solution)/shard_map/ppermute | solution.py:18
  24.4 1.9 copy-start
Sparse Core Ops, SparseCore 0:
  34.0 245.0 all-reduce.1
where the time goes:
time: 339 us
  waiting for transfers between devices  245 us (72%)
  other arithmetic  51.3 us (15%)
  matrix products  14.5 us (4%)
  between operations  14.2 us (4%)
  starting transfers between devices  8.99 us (3%)
  local copies, waits for them, and re-layouts  4.96 us (1%)
    psum x1, waiting for transfers between devices, local(): gram_sum = lax.psum(gram_local, ('gz', 'gx'))  245 us
    another operation x4, other arithmetic, local(): lower = jnp.linalg.cholesky(gram)  23.8 us
    another operation x2, other arithmetic, local(): lax.linalg.triangular_solve(lower, identity_matrix, left_side=True, lower...  19.7 us
    dot_general x1, matrix products, local(): jnp.einsum('pcs,pct->pst', columns, columns, precision=lax.Precision.HIGH...  7.54 us
    ppermute x2, starting transfers between devices, with_halo(): lax.ppermute(head, axis, [((i + 1) % count, i) for i in range(count)])  6.94 us
  transfers between devices with their start and end apart: 5, of which 1 were waited for; matrix products, arithmetic and copies ran while one was open for 1% of the time, Pallas kernels for 0%

commit v1 on v0

--- a/solution.py
+++ b/solution.py
@@ -41,7 +41,7 @@
         precision=lax.Precision.HIGHEST,
         preferred_element_type=jnp.float32,
     )
-    gram_sum = lax.psum(gram_local, ("gz", "gx"))
+    gram_sum = jnp.sum(lax.all_gather(gram_local, ("gz", "gx")), 0)
     total_cells = rows_x * rows_z * lax.axis_size("gz") * lax.axis_size("gx")
     gram = gram_sum / total_cells
     lower = jnp.linalg.cholesky(gram)

time: 339 us -> 257 us (0.76)
  waiting for transfers between devices: 245 us -> 151 us
  other arithmetic: 51.3 us -> 61.8 us
    psum x1 -> x0, waiting for transfers between devices: 245 us -> none  [local(): gram_sum = lax.psum(gram_local, ('gz', 'gx'))]
    all_gather x0 -> x1, waiting for transfers between devices: none -> 151 us  [local(): gram_sum = jnp.sum(lax.all_gather(gram_local, ('gz', 'gx')), 0)]
    reduce_sum x0 -> x1, other arithmetic: none -> 12.2 us  [local(): gram_sum = jnp.sum(lax.all_gather(gram_local, ('gz', 'gx')), 0)]
where the time goes in v1:
time: 257 us; the launch traced here: 255 us
  waiting for transfers between devices  151 us (59%)
  other arithmetic  61.8 us (24%)
  matrix products  14.5 us (6%)
  between operations  14.2 us (6%)
  starting transfers between devices  8.99 us (3%)
  local copies, waits for them, and re-layouts  5.06 us (2%)
    all_gather x1, waiting for transfers between devices, local(): gram_sum = jnp.sum(lax.all_gather(gram_local, ('gz', 'gx')), 0)  151 us
    another operation x4, other arithmetic, local(): lower = jnp.linalg.cholesky(gram)  23.8 us
    another operation x2, other arithmetic, local(): lax.linalg.triangular_solve(lower, identity_matrix, left_side=True, lower...  19.7 us
    reduce_sum x1, other arithmetic, local(): gram_sum = jnp.sum(lax.all_gather(gram_local, ('gz', 'gx')), 0)  12.2 us
    dot_general x1, matrix products, local(): jnp.einsum('pcs,pct->pst', columns, columns, precision=lax.Precision.HIGH...  7.62 us
    ppermute x2, starting transfers between devices, with_halo(): lax.ppermute(head, axis, [((i + 1) % count, i) for i in range(count)])  6.94 us
    dot_general x1, matrix products, local(): jnp.einsum('pcs,pst->pct', columns, inverse_r, precision=lax.Precision.HI...  6.55 us
  transfers between devices with their start and end apart: 5, of which 1 were waited for; matrix products, arithmetic and copies ran while one was open for 1% of the time, Pallas kernels for 0%

profile of v1, /device:TPU:2, one launch (start us, length us, event | category | flops | bytes accessed | tf_op | source)
XLA Modules:
  0.0 255.4 jit_solution(11881680217798394827)
XLA Ops:
  7.2 0.0 copy-start.1
  7.2 0.0 all-gather.3.cloned.1.call-start
  7.2 1.3 fusion.13
  8.5 2.0 collective-permute-start
  10.5 4.0 %collective-permute-start.1 = (bf16[2,64,2,128]{3,2,1,0:T(2,128)(2,1)S(1)}, bf16[2,64,2,128]{3,2,1,0:T(2,128)(2,1)S(1)}, u32[]{:S(2)}, u32[]{:S(2)}) collective-permute-start(bf16[2,64,2,128]{3,2,1,0:T(2,128)(2,1)S(1)} %get-tuple-element.9), channel_id=1, source_target_pairs={{8,0},{16,8},{24,16},{32,24},{40,32},{48,40},{56,48},{64,56},{72,6... | collective-permute-start | bytes 196616 | tf_op jit(solution)/shard_map/ppermute | solution.py:18
  14.5 0.9 fusion.14
  15.4 0.0 collective-permute-start.2
  15.4 2.9 %collective-permute-start.3 = (bf16[2,2,64,128]{3,2,1,0:T(8,128)(2,1)S(1)}, bf16[2,2,64,128]{3,2,1,0:T(8,128)(2,1)S(1)}, u32[]{:S(2)}, u32[]{:S(2)}) collective-permute-start(bf16[2,2,64,128]{3,2,1,0:T(8,128)(2,1)S(1)} %get-tuple-element.11), channel_id=1, source_target_pairs={{1,0},{2,1},{3,2},{4,3},{5,4},{6,5},{7,6},{0,7},{9,8},{10,9},{11,1... | collective-permute-start | bytes 196616 | tf_op jit(solution)/shard_map/ppermute | solution.py:18
  18.4 2.8 %maximum_convert_fusion = f32[2,64,68,128]{3,2,1,0:T(8,128)S(1)} fusion(bf16[2,64,2,128]{3,2,1,0:T(2,128)(2,1)S(1)} %collective-permute-done.1, bf16[2,64,64,128]{3,2,1,0:T(8,128)(2,1)} %param.2, bf16[2,64,2,128]{3,2,1,0:T(2,128)(2,1)S(1)} %collective-permute-done), kind=kLoop, calls=%fused_computation.11 | loop fusion | flops 6684672 | bytes 6684672 | tf_op jit(solution)/shard_map/convert_element_type | solution.py:27
  21.2 0.3 maximum_convert_fusion.1
  21.5 2.8 %fusion.2 = f32[2,64,64,128]{3,2,1,0:T(8,128)S(1)} fusion(f32[2,68,64,128]{3,2,1,0:T(8,128)S(1)} %maximum_convert_fusion.1, f32[2,64,68,128]{3,2,1,0:T(8,128)S(1)} %maximum_convert_fusion), kind=kLoop, calls=%fused_computation.3 | loop fusion | flops 11534336 | bytes 37748736 | tf_op jit(solution)/shard_map/sub | solution.py:35
  24.3 2.0 copy-done
  26.3 7.6 %fusion.15 = f32[2,128,128]{2,1,0:T(8,128)} fusion(f32[2,4096,128]{2,1,0:T(8,128)S(1)} %bitcast.18), kind=kOutput, calls=%fused_computation.28 | convolution fusion | flops 1610612736 | bytes 4325376 | tf_op jit(solution)/shard_map/pcs,pct->pst/dot_general | solution.py:37
  34.0 0.0 all-gather.3.cloned.1.call-update
  34.0 150.8 %all-gather.3.cloned.1.call-done = f32[512,128,128]{2,1,0:T(8,128)} async-done(((f32[2,128,128]{2,1,0:T(8,128)}), f32[512,128,128]{2,1,0:T(8,128)}) %all-gather.3.cloned.1.call-update) | async-done | bytes 33554448 | tf_op jit(solution)/shard_map/all_gather | solution.py:44
  184.9 12.2 %reduce_sum.11 = f32[2,128,128]{2,1,0:T(8,128)S(1)} reduce(f32[256,2,128,128]{3,2,1,0:T(8,128)} %bitcast.20, f32[]{:T(128)} %constant.51.clone.1), dimensions={0}, to_apply=%region_0.0 | reduce | flops 8355840 | bytes 33685508 | tf_op jit(solution)/shard_map/reduce_sum | solution.py:44
  197.1 0.1 copy.11
  197.2 23.6 %custom-call.7 = f32[2,128,128]{2,1,0:T(8,128)S(1)} custom-call(f32[2,128,128]{2,1,0:T(8,128)S(1)} %fusion.9), custom_call_target="Cholesky" | custom-call | tf_op jit(solution)/shard_map/jit(cholesky)/cholesky | solution.py:47
  220.9 0.1 compare_reduce_fusion
  221.0 0.1 fusion.10
  221.1 19.7 %custom-call.8 = f32[2,1,128,128]{2,3,1,0:T(8,128)S(1)} custom-call(f32[2,1,128,128]{3,2,1,0:T(8,128)S(1)} %get-tuple-element.13), custom_call_target="InvertDiagBlocksLowerTriangular" | custom-call | tf_op jit(solution)/shard_map/triangular_solve | solution.py:49
  240.8 0.4 fusion.7
  241.2 6.5 %fusion.16 = f32[2,4096,128]{2,1,0:T(8,128)} fusion(f32[2,4096,128]{2,1,0:T(8,128)} %bitcast.19, f32[2,128,128]{2,1,0:T(8,128)S(1)} %fusion.7), kind=kOutput, calls=%fused_computation.29 | convolution fusion | flops 1610612736 | bytes 8519680 | tf_op jit(solution)/shard_map/pcs,pst->pct/dot_general | solution.py:51
  247.8 0.8 copy.13
  (11 shorter events, 0.1 us)
Async XLA Ops:
  7.2 14.0 %copy-start.1 = (bf16[2,64,64,128]{3,2,1,0:T(8,128)(2,1)S(1)}, bf16[2,64,64,128]{3,2,1,0:T(8,128)(2,1)}, u32[]{:S(2)}) copy-start(bf16[2,64,64,128]{3,2,1,0:T(8,128)(2,1)} %param.3) | copy-start | bytes 6291460
  7.2 177.7 %all-gather.3.cloned.1.call-start = ((), (), s32[]{:S(2)}) async-start(), calls=%async_computation | async-start | bytes 33685504 | tf_op jit(solution)/shard_map/all_gather | solution.py:44
  8.5 9.9 %collective-permute-start = (bf16[2,64,2,128]{3,2,1,0:T(2,128)(2,1)S(1)}, bf16[2,64,2,128]{3,2,1,0:T(2,128)(2,1)S(1)}, u32[]{:S(2)}, u32[]{:S(2)}) collective-permute-start(bf16[2,64,2,128]{3,2,1,0:T(2,128)(2,1)S(1)} %get-tuple-element.8), channel_id=1, source_target_pairs={{0,8},{8,16},{16,24},{24,32},{32,40},{40,48},{48,56},{56,64},{64,7... | collective-permute-start | bytes 196616 | tf_op jit(solution)/shard_map/ppermute | solution.py:16
  10.5 7.9 %collective-permute-start.1 = (bf16[2,64,2,128]{3,2,1,0:T(2,128)(2,1)S(1)}, bf16[2,64,2,128]{3,2,1,0:T(2,128)(2,1)S(1)}, u32[]{:S(2)}, u32[]{:S(2)}) collective-permute-start(bf16[2,64,2,128]{3,2,1,0:T(2,128)(2,1)S(1)} %get-tuple-element.9), channel_id=1, source_target_pairs={{8,0},{16,8},{24,16},{32,24},{40,32},{48,40},{56,48},{64,56},{72,6... | collective-permute-start | bytes 196616 | tf_op jit(solution)/shard_map/ppermute | solution.py:18
  15.4 5.8 %collective-permute-start.2 = (bf16[2,2,64,128]{3,2,1,0:T(8,128)(2,1)S(1)}, bf16[2,2,64,128]{3,2,1,0:T(8,128)(2,1)S(1)}, u32[]{:S(2)}, u32[]{:S(2)}) collective-permute-start(bf16[2,2,64,128]{3,2,1,0:T(8,128)(2,1)S(1)} %get-tuple-element.10), channel_id=1, source_target_pairs={{0,1},{1,2},{2,3},{3,4},{4,5},{5,6},{6,7},{7,0},{8,9},{9,10},{10,1... | collective-permute-start | bytes 196616 | tf_op jit(solution)/shard_map/ppermute | solution.py:16
  15.4 5.7 %collective-permute-start.3 = (bf16[2,2,64,128]{3,2,1,0:T(8,128)(2,1)S(1)}, bf16[2,2,64,128]{3,2,1,0:T(8,128)(2,1)S(1)}, u32[]{:S(2)}, u32[]{:S(2)}) collective-permute-start(bf16[2,2,64,128]{3,2,1,0:T(8,128)(2,1)S(1)} %get-tuple-element.11), channel_id=1, source_target_pairs={{1,0},{2,1},{3,2},{4,3},{5,4},{6,5},{7,6},{0,7},{9,8},{10,9},{11,1... | collective-permute-start | bytes 196616 | tf_op jit(solution)/shard_map/ppermute | solution.py:18
  24.3 2.0 copy-start
Sparse Core Ops, SparseCore 0:
  34.1 150.7 all-gather.2
